TPU v7x, 32 devices: a whole 2x2x4 slice. The times are simulated.
32 devices in a mesh: group: 2 (over y), head: 4 (over x, core), seq: 4 (over z).
Axes of the slice: x: 2, y: 2, z: 4, core: 2. Of those that a mesh axis runs over, the one named last changes fastest.
Arguments:
- new_queries: bfloat16 [512, 4096], P(('group', 'seq'), 'head'), parts along dimension 0, may hold values from -80 to 80
- new_keys: bfloat16 [512, 1024], P(('group', 'seq'), 'head'), parts along dimension 0, may hold values from -6 to 6
- new_values: bfloat16 [512, 1024], P(('group', 'seq'), 'head'), parts along dimension 0, may hold values from -6 to 6
- cache_keys: bfloat16 [8192, 1024], P(('group', 'seq'), 'head'), parts along dimension 0, may hold values from -5 to 5
- cache_values: bfloat16 [8192, 1024], P(('group', 'seq'), 'head'), parts along dimension 0, may hold values from -6 to 6
- segment_ids: int32 [512], P('group'), parts along dimension 0, may hold values from 0 to 7, as said below
- cache_length: int32 [2], P('group'), parts along dimension 0, may hold values from 512 to 4096
Outputs:
- attended: bfloat16 [512, 4096], P(('group', 'seq'), 'head'), parts along dimension 0
There are 2 independent parts, one for each index of `group`. A program takes and returns all parts, laid end to end along the dimension named above; each array names one. Nothing has to cross between parts.
Inputs may be any that keep to these rules, and one draw needn't show every extreme that they name: `segment_ids`: Non-decreasing along the positions; every number of 0 to 7 appears.
All inputs are finite; a program needn't handle non-finite values.
Results may differ from a plain program's by a relative error of at most 0.0024.
Values may be sent and summed in bfloat16 or wider, within the bound.
No kernel may reach another device: no remote copies, remote signals or barrier semaphores. Data moves between devices by JAX's collectives and lax.ppermute only.
A program may use at most 64 MiB of HBM per device.

v0:
```python
import jax
import jax.numpy as jnp
from jax import lax
from jax.sharding import PartitionSpec as P

HEAD_DIM = 128
NEG_FILL = -1e30


def on_device(
    new_queries, new_keys, new_values, cache_keys, cache_values, segment_ids, cache_length
):
    head_size = HEAD_DIM
    own_count = new_queries.shape[0]
    join_rows = segment_ids.shape[0]
    cache_rows = cache_keys.shape[0]
    heads_kv = cache_keys.shape[1] // head_size
    heads_q = new_queries.shape[1] // head_size
    group_size = heads_q // heads_kv
    seq_count = lax.axis_size("seq")
    seq_rank = lax.axis_index("seq")
    score_scale = head_size ** (-0.5)
    cache_limit = cache_length[0]
    all_queries, all_keys, all_values = (
        lax.all_gather(new_queries, "seq", axis=0, tiled=True),
        lax.all_gather(new_keys, "seq", axis=0, tiled=True),
        lax.all_gather(new_values, "seq", axis=0, tiled=True),
    )
    keys_here, values_here = (cache_keys, cache_values)
    live_rows = jnp.clip(cache_limit - seq_rank * cache_rows, 0, cache_rows)
    tile_width = min(cache_rows // seq_count, 256)
    block_rows = min(256, cache_rows)
    tiles_per_block = block_rows // tile_width
    block_total = (live_rows + block_rows - 1) // block_rows
    keys_tiled = keys_here.reshape(cache_rows, heads_kv, head_size)
    values_tiled = values_here.reshape(cache_rows, heads_kv, head_size)
    query_block = min(64, join_rows)
    grouped = all_queries.reshape(
        join_rows // query_block, query_block, heads_kv, group_size, head_size
    )

    def one_block(block_queries):

        def step_pass(block_index, running):
            best, numer_acc, denom_acc = running
            start = block_index * block_rows
            key_tile = lax.dynamic_slice_in_dim(keys_tiled, start, block_rows, 0)
            scores = (
                jnp.einsum(
                    "cgrd,tgd->cgrt", block_queries, key_tile, preferred_element_type=jnp.float32
                )
                * score_scale
            )
            usable = (start + jnp.arange(block_rows, dtype=jnp.int32) < live_rows).reshape(
                tiles_per_block, tile_width
            )
            split = scores.reshape(query_block, heads_kv, group_size, tiles_per_block, tile_width)
            tile_max = jnp.max(jnp.where(usable, split, NEG_FILL), axis=-1)
            weights = jnp.exp(jnp.where(usable, split - tile_max[..., None], NEG_FILL)).astype(
                jnp.bfloat16
            )
            value_tile = lax.dynamic_slice_in_dim(values_tiled, start, block_rows, 0).reshape(
                tiles_per_block, tile_width, heads_kv, head_size
            )
            tile_numer = jnp.einsum(
                "cgrbt,btgd->cgrbd", weights, value_tile, preferred_element_type=jnp.float32
            )
            tile_denom = jnp.sum(weights.astype(jnp.float32), axis=-1)
            new_best = jnp.maximum(best, jnp.max(tile_max, axis=-1))
            keep = jnp.exp(best - new_best)
            factor = jnp.exp(tile_max - new_best[..., None])
            numer_acc = numer_acc * keep[..., None] + jnp.sum(
                tile_numer * factor[..., None], axis=3
            )
            denom_acc = denom_acc * keep + jnp.sum(tile_denom * factor, axis=-1)
            return (new_best, numer_acc, denom_acc)

        start_state = (
            jnp.full((query_block, heads_kv, group_size), NEG_FILL, jnp.float32),
            jnp.zeros((query_block, heads_kv, group_size, head_size), jnp.float32),
            jnp.zeros((query_block, heads_kv, group_size), jnp.float32),
        )
        return lax.fori_loop(0, block_total, step_pass, start_state)

    block_best, block_numer, block_denom = lax.map(one_block, grouped)
    cache_max = block_best.reshape(join_rows, heads_kv, group_size)
    cache_numer = block_numer.reshape(join_rows, heads_kv, group_size, head_size)
    cache_denom = block_denom.reshape(join_rows, heads_kv, group_size)
    own_queries = new_queries.reshape(own_count, heads_kv, group_size, head_size)
    fresh_scores = (
        jnp.einsum(
            "cgrd,tgd->cgrt",
            own_queries,
            all_keys.reshape(join_rows, heads_kv, head_size),
            preferred_element_type=jnp.float32,
        )
        * score_scale
    )
    start_row = seq_rank * own_count
    own_positions = start_row + jnp.arange(own_count, dtype=jnp.int32)
    own_segments = lax.dynamic_slice_in_dim(segment_ids, start_row, own_count, 0)
    key_positions = jnp.arange(join_rows, dtype=jnp.int32)
    allowed = (key_positions[None, :] <= own_positions[:, None]) & (
        segment_ids[None, :] == own_segments[:, None]
    )
    allowed = allowed[:, None, None, :]
    fresh_max = jnp.max(jnp.where(allowed, fresh_scores, NEG_FILL), axis=-1)
    zero_index = jnp.zeros((), jnp.int32)
    merged = lax.dynamic_update_slice(
        cache_max,
        jnp.maximum(lax.dynamic_slice_in_dim(cache_max, start_row, own_count, 0), fresh_max),
        (start_row, zero_index, zero_index),
    )
    row_max = (
        lax.pmax(merged.reshape(join_rows, heads_q).astype(jnp.bfloat16), "seq")
        .astype(jnp.float32)
        .reshape(join_rows, heads_kv, group_size)
    )
    rescale = jnp.exp(cache_max - row_max)
    scaled_numer = (cache_numer * rescale[..., None]).reshape(join_rows, heads_q * head_size)
    scaled_denom = (cache_denom * rescale).reshape(join_rows, heads_q)
    own_numer, own_denom = (
        lax.psum_scatter(scaled_numer, "seq", scatter_dimension=0, tiled=True),
        lax.psum_scatter(scaled_denom, "seq", scatter_dimension=0, tiled=True),
    )
    own_max = lax.dynamic_slice_in_dim(row_max, start_row, own_count, 0)
    fresh_weights = jnp.exp(
        jnp.where(allowed, fresh_scores - fresh_max[..., None], NEG_FILL)
    ).astype(jnp.bfloat16)
    fresh_factor = jnp.exp(fresh_max - own_max)
    fresh_numer = (
        jnp.einsum(
            "cgrt,tgd->cgrd",
            fresh_weights,
            all_values.reshape(join_rows, heads_kv, head_size),
            preferred_element_type=jnp.float32,
        )
        * fresh_factor[..., None]
    )
    fresh_denom = jnp.sum(fresh_weights.astype(jnp.float32), axis=-1) * fresh_factor
    total_numer = own_numer + fresh_numer.reshape(own_count, heads_q * head_size)
    total_denom = own_denom + fresh_denom.reshape(own_count, heads_q)
    attended = total_numer.reshape(own_count, heads_q, head_size) / total_denom[..., None]
    return attended.reshape(own_count, heads_q * head_size).astype(jnp.bfloat16)


def solution(mesh):
    placed = (
        P(("group", "seq"), "head"),
        P(("group", "seq"), "head"),
        P(("group", "seq"), "head"),
        P(("group", "seq"), "head"),
        P(("group", "seq"), "head"),
        P("group"),
        P("group"),
    )
    return jax.shard_map(
        on_device,
        mesh=mesh,
        in_specs=placed,
        out_specs=P(("group", "seq"), "head"),
        check_vma=False,
    )
```

profile of v0, /device:TPU:0, one launch (start us, length us, event | category | flops | bytes accessed | tf_op | source)
XLA Modules:
  0.0 127.6 jit_solution(12809682222911493052)
XLA Ops:
  7.2 17.6 %all_gather.9 = bf16[256,1024]{1,0:T(8,128)(2,1)S(1)} all-gather(bf16[64,1024]{1,0:T(8,128)(2,1)} %param.11), channel_id=1, replica_groups=mesh['group'=2,'head'=4,'seq'=4] {'seq'}, dimensions={0}, use_global_device_ids=true | all-gather | bytes 655360 | tf_op jit(solution)/shard_map/all_gather | solution.py:25
  24.8 0.4 reshape.144
  25.2 0.7 copy-done.1
  26.3 1.3 copy.30
  27.9 18.3 %while.29 = (s32[]{:T(128)}, f32[4,64,2,4]{1,0,3,2:T(4,128)S(1)}, f32[4,64,2,4,128]{4,3,2,1,0:T(4,128)S(1)}, f32[4,64,2,4]{1,0,3,2:T(4,128)S(1)}, bf16[4,64,2,4,...) while((s32[]{:T(128)}, f32[4,64,2,4]{1,0,3,2:T(4,128)S(1)}, ...), condition=%wide.region_5.6_spmd, body=%wide.region_0.5_spmd.sunk | while | flops 68749824 | bytes 3850228 | solution.py:85
  28.0 4.1 %while.30 = (s32[]{:T(128)}, f32[64,2,4]{0,2,1:T(4,128)S(1)}, f32[64,2,4,128]{3,0,2,1:T(8,128)S(1)}, f32[64,2,4]{0,2,1:T(4,128)S(1)}, s32[]{:T(128)}, /*index=5*...) while((s32[]{:T(128)}, f32[64,2,4]{0,2,1:T(4,128)S(1)}, ...), condition=%wide.region_4.4_spmd, body=%wide.region_1.3_spmd.sunk | while | flops 68749824 | bytes 2526915 | solution.py:83
  29.7 0.4 fusion.26
  31.8 0.4 fusion.26
  32.6 4.1 %while.30 = (s32[]{:T(128)}, f32[64,2,4]{0,2,1:T(4,128)S(1)}, f32[64,2,4,128]{3,0,2,1:T(8,128)S(1)}, f32[64,2,4]{0,2,1:T(4,128)S(1)}, s32[]{:T(128)}, /*index=5*...) while((s32[]{:T(128)}, f32[64,2,4]{0,2,1:T(4,128)S(1)}, ...), condition=%wide.region_4.4_spmd, body=%wide.region_1.3_spmd.sunk | while | flops 68749824 | bytes 2526915 | solution.py:83
  33.3 0.4 fusion.26
  35.3 0.4 fusion.26
  37.1 4.1 %while.30 = (s32[]{:T(128)}, f32[64,2,4]{0,2,1:T(4,128)S(1)}, f32[64,2,4,128]{3,0,2,1:T(8,128)S(1)}, f32[64,2,4]{0,2,1:T(4,128)S(1)}, s32[]{:T(128)}, /*index=5*...) while((s32[]{:T(128)}, f32[64,2,4]{0,2,1:T(4,128)S(1)}, ...), condition=%wide.region_4.4_spmd, body=%wide.region_1.3_spmd.sunk | while | flops 68749824 | bytes 2526915 | solution.py:83
  37.8 0.4 fusion.26
  39.9 0.4 fusion.26
  41.7 4.1 %while.30 = (s32[]{:T(128)}, f32[64,2,4]{0,2,1:T(4,128)S(1)}, f32[64,2,4,128]{3,0,2,1:T(8,128)S(1)}, f32[64,2,4]{0,2,1:T(4,128)S(1)}, s32[]{:T(128)}, /*index=5*...) while((s32[]{:T(128)}, f32[64,2,4]{0,2,1:T(4,128)S(1)}, ...), condition=%wide.region_4.4_spmd, body=%wide.region_1.3_spmd.sunk | while | flops 68749824 | bytes 2526915 | solution.py:83
  42.4 0.4 fusion.26
  44.4 0.4 fusion.26
  46.5 0.7 copy-done.3
  47.1 13.3 %all_gather.10 = bf16[256,256]{1,0:T(8,128)(2,1)S(1)} all-gather(bf16[64,256]{1,0:T(8,128)(2,1)S(1)} %copy-done.3), channel_id=1, replica_groups=mesh['group'=2,'head'=4,'seq'=4] {'seq'}, dimensions={0}, use_global_device_ids=true | all-gather | bytes 163840 | tf_op jit(solution)/shard_map/all_gather | solution.py:26
  60.6 0.7 copy-done.5
  62.0 8.7 %pmax.7 = bf16[256,8]{0,1:T(8,128)(2,1)S(1)} all-reduce(bf16[256,8]{0,1:T(8,128)(2,1)S(1)} %convert_element_type.27), channel_id=1, replica_groups=mesh['group'=2,'head'=4,'seq'=4] {'seq'}, use_global_device_ids=true, to_apply=%region_7.8 | all-reduce | flops 2048 | bytes 8192 | tf_op jit(solution)/shard_map/pmax | solution.py:115
  70.7 0.8 copy.54
  71.6 0.4 reshape.147
  72.2 1.6 %mul.74 = f32[256,2,4,128]{3,2,1,0:T(4,128)} broadcast(f32[256,2,4]{2,1,0:T(2,128)S(1)} %copy.39), dimensions={0,1,2} | broadcast | bytes 1056768 | tf_op jit(solution)/shard_map/mul | solution.py:120
  73.8 1.6 %mul.75 = f32[256,1024]{1,0:T(8,128)S(1)} reshape(f32[256,2,4,128]{3,2,1,0:T(4,128)} %mul.74) | data formatting | bytes 2097152 | tf_op jit(solution)/shard_map/mul | solution.py:120
  75.4 1.2 mul.76
  76.6 0.7 copy-done.4
  77.3 13.5 %all_gather.11 = bf16[256,256]{1,0:T(8,128)(2,1)S(1)} all-gather(bf16[64,256]{1,0:T(8,128)(2,1)S(1)} %copy-done.4), channel_id=1, replica_groups=mesh['group'=2,'head'=4,'seq'=4] {'seq'}, dimensions={0}, use_global_device_ids=true | all-gather | bytes 163840 | tf_op jit(solution)/shard_map/all_gather | solution.py:27
  92.0 0.8 copy.55
  92.9 26.2 %reduce-scatter.5.cloned.1.call-done = f32[64,1024]{1,0:T(8,128)} async-done(((f32[256,1024]{1,0:T(8,128)}), f32[64,1024]{1,0:T(8,128)}) %reduce-scatter.5.cloned.1.call-update) | async-done | bytes 262160 | tf_op jit(solution)/shard_map/reduce_scatter | solution.py:123
  119.2 0.8 copy-done.2
  120.0 0.7 fusion.13
  (149 shorter events, 17.8 us)
Async XLA Ops:
  6.5 85.4 %reduce-scatter.7.cloned.1.call-start = ((), (), s32[]{:S(2)}) async-start(), calls=%async_computation.3 | async-start | bytes 163840
  24.8 1.0 copy-start.1
  27.9 18.4 %copy-start = (bf16[64,1024]{1,0:T(8,128)(2,1)S(1)}, bf16[64,1024]{1,0:T(8,128)(2,1)}, u32[]{:S(2)}) copy-start(bf16[64,1024]{1,0:T(8,128)(2,1)} %param.11) | copy-start | bytes 393220
  46.4 0.8 copy-start.3
  60.6 0.7 copy-start.5
  71.5 47.6 %reduce-scatter.5.cloned.1.call-start = ((), (), s32[]{:S(2)}) async-start(), calls=%async_computation.2 | async-start | bytes 1310720 | tf_op jit(solution)/shard_map/reduce_scatter | solution.py:123
  76.6 0.8 copy-start.4
  119.1 0.9 copy-start.2
Sparse Core Ops, SparseCore 0:
  71.6 19.7 reduce-scatter.6
  93.8 25.1 reduce-scatter.4
where the time goes:
time: 128 us
  blocking collectives  53.1 us (41%)
  waiting for transfers between devices  26.3 us (21%)
  between operations  14.3 us (11%)
  local copies, waits for them, and re-layouts  14.1 us (11%)
  matrix products  11.4 us (9%)
  other arithmetic  7.33 us (6%)
    reduce_scatter x1, waiting for transfers between devices, on_device(): lax.psum_scatter(scaled_numer, 'seq', scatter_dimension=0, tiled=True)  26.2 us
    all_gather x1, blocking collectives, on_device(): lax.all_gather(new_queries, 'seq', axis=0, tiled=True)  17.6 us
    all_gather x1, blocking collectives, on_device(): lax.all_gather(new_values, 'seq', axis=0, tiled=True)  13.5 us
    all_gather x1, blocking collectives, on_device(): lax.all_gather(new_keys, 'seq', axis=0, tiled=True)  13.3 us
    pmax x1, blocking collectives, on_device(): lax.pmax(merged.reshape(join_rows, heads_q).astype(jnp.bfloat16), 'seq')  8.67 us
    unnamed x17, local copies, waits for them, and re-layouts  6.63 us
    dot_general x16, matrix products, step_pass(): jnp.einsum('cgrbt,btgd->cgrbd', weights, value_tile, preferred_element_ty...  5.59 us
    dot_general x16, matrix products, step_pass(): jnp.einsum('cgrd,tgd->cgrt', block_queries, key_tile, preferred_element_t...  5.24 us
  transfers between devices with their start and end apart: 2, of which 1 were waited for; matrix products, arithmetic and copies ran while one was open for 5% of the time, Pallas kernels for 0%

commit v1 on v0

--- a/solution.py
+++ b/solution.py
@@ -5,6 +5,20 @@
 
 HEAD_DIM = 128
 NEG_FILL = -1e30
+
+
+def turn_bars(base_x):
+    link_axis = "seq"
+    ledger = [base_x]
+    n_slots = jax.lax.axis_size(link_axis)
+    for rr in range(1, n_slots):
+        outer = jax.lax.ppermute(
+            ledger[rr - 1], link_axis, [(u, (u - 1) % n_slots) for u in range(n_slots)]
+        )
+        ledger.append(outer)
+    high = jnp.concatenate(ledger, 0)
+    after = jnp.roll(high, jax.lax.axis_index(link_axis) * base_x.shape[0], 0)
+    return after
 
 
 def on_device(
@@ -23,7 +37,7 @@
     cache_limit = cache_length[0]
     all_queries, all_keys, all_values = (
         lax.all_gather(new_queries, "seq", axis=0, tiled=True),
-        lax.all_gather(new_keys, "seq", axis=0, tiled=True),
+        turn_bars(new_keys),
         lax.all_gather(new_values, "seq", axis=0, tiled=True),
     )
     keys_here, values_here = (cache_keys, cache_values)

time: 128 us -> 130 us (1.016)
  blocking collectives: 53.1 us -> 42.2 us
  starting transfers between devices: 0.04 us -> 7.48 us
  waiting for transfers between devices: 26.3 us -> 29.1 us
  local copies, waits for them, and re-layouts: 14.1 us -> 16.1 us
    all_gather x1 -> x0, blocking collectives: 13.3 us -> none  [on_device(): lax.all_gather(new_keys, 'seq', axis=0, tiled=True)]
    ppermute x0 -> x3, starting transfers between devices: none -> 7.44 us  [turn_bars(): jax.lax.ppermute(ledger[rr - 1], link_axis, [(u, (u - 1) % n_slots) for u...]
    ppermute x0 -> x3, waiting for transfers between devices: none -> 4.61 us  [turn_bars(): jax.lax.ppermute(ledger[rr - 1], link_axis, [(u, (u - 1) % n_slots) for u...]
    pmax x1, blocking collectives: 8.67 us -> 12.8 us  [on_device(): lax.pmax(merged.reshape(join_rows, heads_q).astype(jnp.bfloat16), 'seq')]
    reduce_scatter x1, waiting for transfers between devices: 26.2 us -> 24.4 us  [on_device(): lax.psum_scatter(scaled_numer, 'seq', scatter_dimension=0, tiled=True)]
    all_gather x1, blocking collectives: 17.6 us -> 15.9 us  [on_device(): lax.all_gather(new_queries, 'seq', axis=0, tiled=True)]
    unnamed x17 -> x18, local copies, waits for them, and re-layouts: 6.63 us -> 7.49 us
  transfers between devices with their start and end apart: 2 -> 5, of which waited for: 1 -> 3; matrix products, arithmetic and copies ran while one was open for 5% -> 21% of each run, Pallas kernels for 0% -> 0%
where the time goes in v1:
time: 130 us; the launch traced here: 129 us
  blocking collectives  42.2 us (32%)
  waiting for transfers between devices  29.1 us (22%)
  local copies, waits for them, and re-layouts  16.1 us (12%)
  between operations  14.3 us (11%)
  matrix products  11.4 us (9%)
  starting transfers between devices  7.48 us (6%)
  other arithmetic  7.35 us (6%)
    reduce_scatter x1, waiting for transfers between devices, on_device(): lax.psum_scatter(scaled_numer, 'seq', scatter_dimension=0, tiled=True)  24.4 us
    all_gather x1, blocking collectives, on_device(): lax.all_gather(new_queries, 'seq', axis=0, tiled=True)  15.9 us
    all_gather x1, blocking collectives, on_device(): lax.all_gather(new_values, 'seq', axis=0, tiled=True)  13.5 us
    pmax x1, blocking collectives, on_device(): lax.pmax(merged.reshape(join_rows, heads_q).astype(jnp.bfloat16), 'seq')  12.8 us
    unnamed x18, local copies, waits for them, and re-layouts  7.49 us
    ppermute x3, starting transfers between devices, turn_bars(): jax.lax.ppermute(ledger[rr - 1], link_axis, [(u, (u - 1) % n_slots) for u...  7.44 us
    dot_general x16, matrix products, step_pass(): jnp.einsum('cgrbt,btgd->cgrbd', weights, value_tile, preferred_element_ty...  5.59 us
    dot_general x16, matrix products, step_pass(): jnp.einsum('cgrd,tgd->cgrt', block_queries, key_tile, preferred_element_t...  5.24 us
  transfers between devices with their start and end apart: 5, of which 3 were waited for; matrix products, arithmetic and copies ran while one was open for 21% of the time, Pallas kernels for 0%

profile of v1, /device:TPU:0, one launch (start us, length us, event | category | flops | bytes accessed | tf_op | source)
XLA Modules:
  0.0 129.0 jit_solution(10030864608924794815)
XLA Ops:
  6.5 1.5 %copy.39 = bf16[64,256]{0,1:T(8,128)(2,1)} copy(bf16[64,256]{1,0:T(8,128)(2,1)} %param.12) | data formatting | bytes 65536 | tf_op args[1]
  8.1 5.0 %collective-permute-start = (bf16[64,256]{0,1:T(8,128)(2,1)}, bf16[64,256]{0,1:T(8,128)(2,1)S(1)}, u32[]{:S(2)}, u32[]{:S(2)}) collective-permute-start(bf16[64,256]{0,1:T(8,128)(2,1)} %copy.39), channel_id=1, source_target_pairs={{0,3},{1,0},{2,1},{3,2},{4,7},{5,4},{6,5},{7,6},{8,11},{9,8},{10,9... | collective-permute-start | bytes 98312 | tf_op jit(solution)/shard_map/ppermute | solution.py:15
  13.8 15.9 %all_gather.6 = bf16[256,1024]{1,0:T(8,128)(2,1)S(1)} all-gather(bf16[64,1024]{1,0:T(8,128)(2,1)S(1)} %copy-done), channel_id=1, replica_groups=mesh['group'=2,'head'=4,'seq'=4] {'seq'}, dimensions={0}, use_global_device_ids=true | all-gather | bytes 655360 | tf_op jit(solution)/shard_map/all_gather | solution.py:39
  29.7 0.4 reshape.144
  30.1 0.7 copy-done.2
  31.2 1.3 copy.32
  32.8 18.3 %while.29 = (s32[]{:T(128)}, f32[4,64,2,4]{1,0,3,2:T(4,128)S(1)}, f32[4,64,2,4,128]{4,3,2,1,0:T(4,128)S(1)}, f32[4,64,2,4]{1,0,3,2:T(4,128)S(1)}, bf16[4,64,2,4,...) while((s32[]{:T(128)}, f32[4,64,2,4]{1,0,3,2:T(4,128)S(1)}, ...), condition=%wide.region_5.6_spmd, body=%wide.region_0.5_spmd.sunk | while | flops 68749824 | bytes 3850228 | solution.py:99
  32.9 4.1 %while.30 = (s32[]{:T(128)}, f32[64,2,4]{0,2,1:T(4,128)S(1)}, f32[64,2,4,128]{3,0,2,1:T(8,128)S(1)}, f32[64,2,4]{0,2,1:T(4,128)S(1)}, s32[]{:T(128)}, /*index=5*...) while((s32[]{:T(128)}, f32[64,2,4]{0,2,1:T(4,128)S(1)}, ...), condition=%wide.region_4.4_spmd, body=%wide.region_1.3_spmd.sunk | while | flops 68749824 | bytes 2526915 | solution.py:97
  37.5 4.1 %while.30 = (s32[]{:T(128)}, f32[64,2,4]{0,2,1:T(4,128)S(1)}, f32[64,2,4,128]{3,0,2,1:T(8,128)S(1)}, f32[64,2,4]{0,2,1:T(4,128)S(1)}, s32[]{:T(128)}, /*index=5*...) while((s32[]{:T(128)}, f32[64,2,4]{0,2,1:T(4,128)S(1)}, ...), condition=%wide.region_4.4_spmd, body=%wide.region_1.3_spmd.sunk | while | flops 68749824 | bytes 2526915 | solution.py:97
  38.1 0.4 fusion.26
  40.2 0.4 fusion.26
  42.0 4.1 %while.30 = (s32[]{:T(128)}, f32[64,2,4]{0,2,1:T(4,128)S(1)}, f32[64,2,4,128]{3,0,2,1:T(8,128)S(1)}, f32[64,2,4]{0,2,1:T(4,128)S(1)}, s32[]{:T(128)}, /*index=5*...) while((s32[]{:T(128)}, f32[64,2,4]{0,2,1:T(4,128)S(1)}, ...), condition=%wide.region_4.4_spmd, body=%wide.region_1.3_spmd.sunk | while | flops 68749824 | bytes 2526915 | solution.py:97
  42.7 0.4 fusion.26
  46.6 4.1 %while.30 = (s32[]{:T(128)}, f32[64,2,4]{0,2,1:T(4,128)S(1)}, f32[64,2,4,128]{3,0,2,1:T(8,128)S(1)}, f32[64,2,4]{0,2,1:T(4,128)S(1)}, s32[]{:T(128)}, /*index=5*...) while((s32[]{:T(128)}, f32[64,2,4]{0,2,1:T(4,128)S(1)}, ...), condition=%wide.region_4.4_spmd, body=%wide.region_1.3_spmd.sunk | while | flops 68749824 | bytes 2526915 | solution.py:97
  47.3 0.4 fusion.26
  51.1 0.7 copy-done.5
  51.9 3.5 %collective-permute-done.1 = bf16[64,256]{0,1:T(8,128)(2,1)S(1)} collective-permute-done((bf16[64,256]{0,1:T(8,128)(2,1)S(1)}, bf16[64,256]{0,1:T(8,128)(2,1)S(1)}, u32[]{:S(2)}, u32[]{:S(2)}) %collective-permute-start.1) | collective-permute-done | bytes 32800 | tf_op jit(solution)/shard_map/ppermute | solution.py:15
  55.3 2.3 %collective-permute-start.2 = (bf16[64,256]{0,1:T(8,128)(2,1)S(1)}, bf16[64,256]{0,1:T(8,128)(2,1)S(1)}, u32[]{:S(2)}, u32[]{:S(2)}) collective-permute-start(bf16[64,256]{0,1:T(8,128)(2,1)S(1)} %collective-permute-done.1), channel_id=1, source_target_pairs={{0,3},{1,0},{2,1},{3,2},{4,7},{5,4},{6,5},{7,6},{8,11},{9,8},{10,9... | collective-permute-start | bytes 98312 | tf_op jit(solution)/shard_map/ppermute | solution.py:15
  58.1 0.4 reshape.147
  58.5 1.1 collective-permute-done.2
  59.7 1.1 concatenate.6
  61.4 12.8 %pmax.7 = bf16[256,8]{0,1:T(8,128)(2,1)S(1)} all-reduce(bf16[256,8]{0,1:T(8,128)(2,1)S(1)} %convert_element_type.27), channel_id=1, replica_groups=mesh['group'=2,'head'=4,'seq'=4] {'seq'}, use_global_device_ids=true, to_apply=%region_7.8 | all-reduce | flops 2048 | bytes 8192 | tf_op jit(solution)/shard_map/pmax | solution.py:129
  74.3 0.8 copy.58
  75.3 1.6 %mul.75 = f32[256,2,4,128]{3,2,1,0:T(4,128)} broadcast(f32[256,2,4]{2,1,0:T(2,128)S(1)} %copy.43), dimensions={0,1,2} | broadcast | bytes 1056768 | tf_op jit(solution)/shard_map/mul | solution.py:134
  76.9 1.6 %mul.76 = f32[256,1024]{1,0:T(8,128)S(1)} reshape(f32[256,2,4,128]{3,2,1,0:T(4,128)} %mul.75) | data formatting | bytes 2097152 | tf_op jit(solution)/shard_map/mul | solution.py:134
  78.6 1.2 mul.77
  79.8 0.7 copy-done.4
  80.5 13.5 %all_gather.7 = bf16[256,256]{1,0:T(8,128)(2,1)S(1)} all-gather(bf16[64,256]{1,0:T(8,128)(2,1)S(1)} %copy-done.4), channel_id=1, replica_groups=mesh['group'=2,'head'=4,'seq'=4] {'seq'}, dimensions={0}, use_global_device_ids=true | all-gather | bytes 163840 | tf_op jit(solution)/shard_map/all_gather | solution.py:41
  95.1 0.8 copy.59
  96.0 24.4 %reduce-scatter.5.cloned.1.call-done = f32[64,1024]{1,0:T(8,128)} async-done(((f32[256,1024]{1,0:T(8,128)}), f32[64,1024]{1,0:T(8,128)}) %reduce-scatter.5.cloned.1.call-update) | async-done | bytes 262160 | tf_op jit(solution)/shard_map/reduce_scatter | solution.py:137
  120.6 0.8 copy-done.3
  121.4 0.7 fusion.13
  (156 shorter events, 19.3 us)
Async XLA Ops:
  6.5 7.2 %copy-start = (bf16[64,1024]{1,0:T(8,128)(2,1)S(1)}, bf16[64,1024]{1,0:T(8,128)(2,1)}, u32[]{:S(2)}) copy-start(bf16[64,1024]{1,0:T(8,128)(2,1)} %param.11) | copy-start | bytes 393220
  6.5 88.6 %reduce-scatter.7.cloned.1.call-start = ((), (), s32[]{:S(2)}) async-start(), calls=%async_computation.3 | async-start | bytes 163840
  8.1 43.0 %collective-permute-start = (bf16[64,256]{0,1:T(8,128)(2,1)}, bf16[64,256]{0,1:T(8,128)(2,1)S(1)}, u32[]{:S(2)}, u32[]{:S(2)}) collective-permute-start(bf16[64,256]{0,1:T(8,128)(2,1)} %copy.39), channel_id=1, source_target_pairs={{0,3},{1,0},{2,1},{3,2},{4,7},{5,4},{6,5},{7,6},{8,11},{9,8},{10,9... | collective-permute-start | bytes 98312 | tf_op jit(solution)/shard_map/ppermute | solution.py:15
  29.7 1.0 copy-start.2
  32.7 25.2 %copy-start.1 = (bf16[64,1024]{1,0:T(8,128)(2,1)S(1)}, bf16[64,1024]{1,0:T(8,128)(2,1)}, u32[]{:S(2)}) copy-start(bf16[64,1024]{1,0:T(8,128)(2,1)} %param.11) | copy-start | bytes 393220
  51.0 4.3 %collective-permute-start.1 = (bf16[64,256]{0,1:T(8,128)(2,1)S(1)}, bf16[64,256]{0,1:T(8,128)(2,1)S(1)}, u32[]{:S(2)}, u32[]{:S(2)}) collective-permute-start(bf16[64,256]{0,1:T(8,128)(2,1)S(1)} %collective-permute-done), channel_id=1, source_target_pairs={{0,3},{1,0},{2,1},{3,2},{4,7},{5,4},{6,5},{7,6},{8,11},{9,8},{10,9... | collective-permute-start | bytes 98312 | tf_op jit(solution)/shard_map/ppermute | solution.py:15
  51.1 0.7 copy-start.5
  55.3 4.3 %collective-permute-start.2 = (bf16[64,256]{0,1:T(8,128)(2,1)S(1)}, bf16[64,256]{0,1:T(8,128)(2,1)S(1)}, u32[]{:S(2)}, u32[]{:S(2)}) collective-permute-start(bf16[64,256]{0,1:T(8,128)(2,1)S(1)} %collective-permute-done.1), channel_id=1, source_target_pairs={{0,3},{1,0},{2,1},{3,2},{4,7},{5,4},{6,5},{7,6},{8,11},{9,8},{10,9... | collective-permute-start | bytes 98312 | tf_op jit(solution)/shard_map/ppermute | solution.py:15
  75.1 45.4 %reduce-scatter.5.cloned.1.call-start = ((), (), s32[]{:S(2)}) async-start(), calls=%async_computation.2 | async-start | bytes 1310720 | tf_op jit(solution)/shard_map/reduce_scatter | solution.py:137
  79.8 0.8 copy-start.4
  120.4 0.9 copy-start.3
Sparse Core Ops, SparseCore 0:
  75.2 17.4 reduce-scatter.6
  95.1 25.3 reduce-scatter.4
